TPU v7x, 512 devices: a whole 4x8x8 slice. The times are simulated.
512 devices in a mesh: seq: 64 (over x, z, core), kvh: 4 (over y_hi), rep: 2 (over y_lo).
Axes of the slice: x: 4, y: 8 (y_hi: 4, y_lo: 2; y = y_hi * 2 + y_lo), z: 8, core: 2. Of those that a mesh axis runs over, the one named last changes fastest.
Arguments:
- vision_states: bfloat16 [64, 384, 1152], P('seq', 'kvh'), may hold values from -24 to 24
- frame_tokens: int32 [64], replicated, may hold values from 128 to 384, as said below
- norm_gain: float32 [1152], replicated, may hold values from 0.1 to 1.9
- projector: bfloat16 [1152, 3584], P(None, ('kvh', 'rep')), may hold values from -0.1875 to 0.1875
- head_weights: bfloat16 [3584, 3072], P(('kvh', 'rep')), may hold values from -4 to 4
Outputs:
- attended: bfloat16 [256, 64, 2048], P(None, 'seq', ('kvh', 'rep'))
Inputs may be any that keep to these rules, and one draw needn't show every extreme that they name: `frame_tokens`: the counts sum to 16384, and some frame has exactly 384 tokens.
All inputs are finite; a program needn't handle non-finite values.
Results may differ from a plain program's by a relative error of at most 0.0062.
Values may be sent and summed in bfloat16 or wider, within the bound.
No kernel may reach another device: no remote copies, remote signals or barrier semaphores. Data moves between devices by JAX's collectives and lax.ppermute only.
A program may use at most 128 MiB of HBM per device.

v0:
```python
import jax
import jax.numpy as jnp
from jax import lax
from jax.sharding import PartitionSpec as P

KV_HEADS = 4
HEAD_DIM = 128
GROUP_HEADS = 4
norm_eps = 1e-06
masked_score = -1e30


def layer_norm(states, norm_gain):
    values = states.astype(jnp.float32)
    center = values - jnp.mean(values, axis=-1, keepdims=True)
    spread = jnp.mean(center * center, axis=-1, keepdims=True)
    return (center * lax.rsqrt(spread + norm_eps) * norm_gain).astype(jnp.bfloat16)


def attention_step(queries, query_pos, key_rows, key_base, seq_count):
    scale = queries.shape[-1] ** (-0.5)

    def add_keys(carry, piece, start):
        context, top, total = carry
        key_piece, value_piece = piece
        number = key_piece.shape[0]
        index = jnp.arange(number, dtype=jnp.int32)
        key_pos = (key_base + index % key_rows) * seq_count + index // key_rows
        allowed = (key_pos[None, :] <= query_pos[:, None])[:, None, :]
        scores = (
            jnp.einsum("qhd,kd->qhk", queries, key_piece, preferred_element_type=jnp.float32)
            * scale
        )
        scores = jnp.where(allowed, scores, masked_score)
        new_top = jnp.maximum(top, jnp.max(scores, axis=-1))
        weights = jnp.where(allowed, jnp.exp(scores - new_top[..., None]), 0.0)
        total = jnp.sum(weights, axis=-1)
        update = jnp.einsum(
            "qhk,kd->qhd",
            weights.astype(jnp.bfloat16),
            value_piece,
            preferred_element_type=jnp.float32,
        )
        return (update, new_top, total)

    return add_keys


def empty_partials(tok_rows, head_count):
    return (
        jnp.zeros((tok_rows, head_count, HEAD_DIM), jnp.float32),
        jnp.full((tok_rows, head_count), masked_score, jnp.float32),
        jnp.zeros((tok_rows, head_count), jnp.float32),
    )


def local(vision_states, frame_tokens, norm_gain, projector, head_weights):
    seq_count = lax.axis_size("seq")
    seq_index = lax.axis_index("seq")
    rep_count = lax.axis_size("rep")
    frames_dev = vision_states.shape[0]
    frame_max = vision_states.shape[1] * lax.axis_size("kvh")
    d_cols = projector.shape[1]
    cap_frame = frame_max // seq_count
    tok_rows = 2 * frames_dev * frame_max // 3
    heads_local = GROUP_HEADS // rep_count
    normed = layer_norm(vision_states, norm_gain)
    hidden = jnp.einsum(
        "frv,vc->frc",
        lax.all_gather(normed, "kvh", axis=1, tiled=True),
        projector,
        preferred_element_type=jnp.float32,
    )
    visual_frames = jax.nn.gelu(hidden, approximate=False).astype(jnp.bfloat16)
    ends = jnp.cumsum(frame_tokens)
    starts_all = ends - frame_tokens
    my_starts = lax.dynamic_slice_in_dim(starts_all, seq_index * frames_dev, frames_dev, 0)
    dest = jnp.arange(seq_count, dtype=jnp.int32)[:, None, None]
    slots = jnp.arange(cap_frame, dtype=jnp.int32)[None, None, :]
    frame_local = jnp.arange(frames_dev, dtype=jnp.int32)[None, :, None]
    row_of = jnp.mod(dest - my_starts[None, :, None], seq_count) + slots * seq_count
    send_index = (frame_local * frame_max + row_of).reshape(-1)
    outgoing = visual_frames.reshape(frames_dev * frame_max, d_cols)[send_index]
    received = lax.all_to_all(outgoing, "seq", split_axis=0, concat_axis=0, tiled=True)
    query_pos = jnp.arange(tok_rows, dtype=jnp.int32) * seq_count + seq_index
    before = ends[None, :] <= query_pos[:, None]
    frame = jnp.sum(before.astype(jnp.int32), axis=1)
    offset = jnp.sum(jnp.where(before, frame_tokens[None, :], 0), axis=1)
    slot_index = frame * cap_frame + (query_pos - offset) // seq_count
    visual = received[slot_index]
    wide = head_weights.reshape(d_cols, KV_HEADS, GROUP_HEADS + 2, HEAD_DIM)
    query_w = wide[:, :, :GROUP_HEADS].reshape(d_cols, KV_HEADS, rep_count, heads_local * HEAD_DIM)
    pair_w = wide[:, :, GROUP_HEADS:].reshape(d_cols, KV_HEADS, 1, 2 * HEAD_DIM)
    pair_w = jnp.broadcast_to(pair_w, (d_cols, KV_HEADS, rep_count, 2 * HEAD_DIM))
    piece_w = jnp.concatenate([query_w, pair_w], axis=3).reshape(
        d_cols, KV_HEADS * rep_count, (heads_local + 2) * HEAD_DIM
    )
    summed = lax.psum_scatter(
        jnp.einsum("tc,cpw->ptw", visual, piece_w, preferred_element_type=jnp.float32),
        ("kvh", "rep"),
        scatter_dimension=0,
        tiled=True,
    )[0]
    head_rows = summed.astype(jnp.bfloat16)
    queries = head_rows[:, : heads_local * HEAD_DIM].reshape(tok_rows, heads_local, HEAD_DIM)
    key_own = head_rows[:, heads_local * HEAD_DIM : (heads_local + 1) * HEAD_DIM]
    value_own = head_rows[:, (heads_local + 1) * HEAD_DIM :]
    add_keys = attention_step(queries, query_pos, tok_rows, 0, seq_count)
    context, top, total = add_keys(
        empty_partials(tok_rows, heads_local),
        (
            lax.all_gather(key_own, "seq", axis=0, tiled=True),
            lax.all_gather(value_own, "seq", axis=0, tiled=True),
        ),
        jnp.int32(0),
    )
    result = (context / total[..., None]).astype(jnp.bfloat16)
    return result.reshape(tok_rows, 1, heads_local * HEAD_DIM)


def solution(mesh):
    placed = (P("seq", "kvh", None), P(), P(), P(None, ("kvh", "rep")), P(("kvh", "rep"), None))
    return jax.shard_map(
        local, mesh=mesh, in_specs=placed, out_specs=P(None, "seq", ("kvh", "rep")), check_vma=False
    )
```

profile of v0, /device:TPU:1, one launch (start us, length us, event | category | flops | bytes accessed | tf_op | source)
XLA Modules:
  0.0 328.2 jit_solution(847766380383886331)
XLA Ops:
  6.5 0.0 copy-start
  6.5 0.8 copy.27
  7.4 0.1 reduce-window.8
  7.5 0.1 reduce.2
  7.6 0.7 sub.59
  8.2 0.6 dynamic_slice.3
  8.8 0.7 and_select_fusion.1
  9.5 0.1 broadcast_add_fusion
  9.6 0.1 add.150
  9.7 1.1 convert_reduce_fusion
  10.8 1.2 fusion.42
  12.0 1.1 fusion.44
  13.1 22.0 %all_gather.9 = bf16[1,384,1152]{2,1,0:T(8,128)(2,1)S(1)} all-gather(bf16[1,96,1152]{2,1,0:T(8,128)(2,1)S(1)} %fusion.44), channel_id=1, replica_groups=mesh['seq'=64,'kvh'=4,'rep'=2] {'kvh'}, dimensions={1}, use_global_device_ids=true | all-gather | bytes 1105920 | tf_op jit(solution)/shard_map/all_gather | solution.py:70
  35.2 0.0 copy-done
  35.2 2.1 fusion.30
  37.3 0.2 copy.28
  37.5 2.1 gather_fusion
  39.5 1.0 all_to_all.8
  40.5 16.4 %all-to-all-start = ((bf16[64,6,448]{2,1,0:T(8,128)(2,1)}), bf16[64,6,448]{2,1,0:T(8,128)(2,1)S(1)}, u32[]{:S(2)}, u32[]{:S(2)}) async-start(bf16[64,6,448]{2,1,0:T(8,128)(2,1)} %all_to_all.8), calls=%async_computation | async-start | bytes 1048576 | tf_op jit(solution)/shard_map/all_to_all | solution.py:84
  57.0 0.0 reduce-scatter.2.cloned.1.call-start
  57.0 0.0 copy-start.2
  57.1 4.6 %copy.23 = bf16[448,3072]{0,1:T(8,128)(2,1)} copy(bf16[448,3072]{1,0:T(8,128)(2,1)} %param.9) | data formatting | bytes 5505024 | tf_op args[4]
  61.6 1.8 slice.24
  63.4 2.3 slice.25
  65.7 2.3 copy.26
  68.1 1.5 copy.25
  69.5 0.0 copy-done.2
  69.5 0.1 fusion.53
  69.7 4.6 %all-to-all-done = bf16[64,6,448]{2,1,0:T(8,128)(2,1)S(1)} async-done(((bf16[64,6,448]{2,1,0:T(8,128)(2,1)}), bf16[64,6,448]{2,1,0:T(8,128)(2,1)S(1)}, u32[]{:S(2)}, u32[]{:S(2)}) %all-to-all-start) | async-done | bytes 344096 | tf_op jit(solution)/shard_map/all_to_all | solution.py:84
  74.3 0.2 all_to_all.10
  74.5 1.2 gather_fusion.1
  75.7 0.1 broadcast_in_dim.58
  75.8 4.8 %fusion.13 = f32[8,256,512]{1,2,0:T(8,128)} fusion(bf16[448,8,256]{2,0,1:T(8,128)(2,1)S(1)} %bitcast.45, bf16[448,8,256]{2,0,1:T(8,128)(2,1)} %copy.26, bf16[256,448]{1,0:T(8,128)(2,1)S(1)} %gather_fusion.1), kind=kOutput, calls=%fused_computation.17 | convolution fusion | flops 946864128 | bytes 8093696 | tf_op jit(solution)/shard_map/tc,cpw->ptw/dot_general | solution.py:99
  80.6 0.0 reduce-scatter.2.cloned.1.call-update
  80.6 0.0 all-gather.3.cloned.1.call-start
  80.7 51.4 %reduce-scatter.2.cloned.1.call-done = f32[1,256,512]{1,2,0:T(8,128)} async-done(((f32[8,256,512]{1,2,0:T(8,128)}), f32[1,256,512]{1,2,0:T(8,128)}) %reduce-scatter.2.cloned.1.call-update) | async-done | bytes 524304 | tf_op jit(solution)/shard_map/reduce_scatter | solution.py:98
  132.1 1.1 convert_bitcast_fusion
  133.1 0.7 fusion.63
  133.8 0.0 all-gather.3.cloned.1.call-update
  133.8 0.0 all-gather.5.cloned.1.call-start
  133.9 0.7 all-gather.5.cloned.1.call-update
  134.6 4.3 %broadcast_compare_fusion = pred[256,16384]{1,0:T(8,128)(4,1)} fusion(s32[16384]{0:T(1024)S(1)} %fusion.54, s32[256]{0:T(256)S(1)} %multiply_add_fusion), kind=kLoop, calls=%fused_computation.9 | loop fusion | flops 4194304 | bytes 4260864 | tf_op jit(solution)/shard_map/le | solution.py:29
  138.9 78.7 %all-gather.3.cloned.1.call-done = bf16[16384,128]{0,1:T(8,128)(2,1)} async-done(((bf16[256,128]{0,1:T(8,128)(2,1)}), bf16[16384,128]{0,1:T(8,128)(2,1)}) %all-gather.3.cloned.1.call-update) | async-done | bytes 4194320 | tf_op jit(solution)/shard_map/all_gather | solution.py:112
  217.6 17.6 %fusion = (f32[256,2]{0,1:T(2,128)S(1)}, f32[256,2,16384]{2,0,1:T(8,128)}) fusion(pred[256,16384]{1,0:T(8,128)(4,1)} %broadcast_compare_fusion, bf16[256,2,128]{0,2,1:T(8,128)(2,1)S(1)} %bitcast.46, bf16[16384,128]{0,1:T(8,128)(2,1)} %all-gather.3.cloned.1.call-done), kind=kOutput, calls=%fused_computation.4 | convolution fusion | flops 2172648960 | bytes 42076160 | tf_op jit(solution)/shard_map/qhd,kd->qhk/dot_general | solution.py:31
  235.2 16.3 %fusion.1 = f32[256,2]{0,1:T(2,128)S(1)} fusion(f32[256,2,16384]{2,0,1:T(8,128)} %get-tuple-element.10, f32[256,2]{0,1:T(2,128)S(1)} %broadcast_maximum_fusion, pred[256,16384]{1,0:T(8,128)(4,1)} %broadcast_compare_fusion), kind=kLoop, calls=%fused_computation.5 | loop fusion | flops 41942528 | bytes 37752832 | tf_op jit(solution)/shard_map/reduce_sum | solution.py:37
  251.5 50.8 %all-gather.5.cloned.1.call-done = bf16[16384,128]{0,1:T(8,128)(2,1)} async-done(((bf16[256,128]{0,1:T(8,128)(2,1)}), bf16[16384,128]{0,1:T(8,128)(2,1)}) %all-gather.5.cloned.1.call-update) | async-done | bytes 4194320 | tf_op jit(solution)/shard_map/all_gather | solution.py:113
  302.3 0.0 copy-start.1
  302.3 18.5 %fusion.21 = bf16[256,2,128]{0,2,1:T(8,128)(2,1)S(1)} fusion(bf16[16384,128]{0,1:T(8,128)(2,1)} %all-gather.5.cloned.1.call-done, f32[256,2,16384]{2,0,1:T(8,128)} %get-tuple-element.10, f32[256,2]{0,1:T(2,128)S(1)} %broadcast_maximum_fusion, pred[256,16384]{1,0:T(8,128)(4,1)} %broadcast_compare_fusion, f32[256,2]{0,1:T(2,128)S(1)} %fusion.1), kind=kOutput, calls=%fused_computation.19 | convolution fusion | flops 2189557760 | bytes 42078208 | tf_op jit(solution)/shard_map/qhk,kd->qhd/dot_general | solution.py:38
  320.9 0.8 copy.32
  321.6 0.0 copy-done.1
  (12 shorter events, 0.1 us)
Async XLA Ops:
  6.5 28.6 %copy-start = (bf16[1152,448]{0,1:T(8,128)(2,1)S(1)}, bf16[1152,448]{0,1:T(8,128)(2,1)}, u32[]{:S(2)}) copy-start(bf16[1152,448]{0,1:T(8,128)(2,1)} %param.8) | copy-start | bytes 3096580
  40.5 33.8 %all-to-all-start = ((bf16[64,6,448]{2,1,0:T(8,128)(2,1)}), bf16[64,6,448]{2,1,0:T(8,128)(2,1)S(1)}, u32[]{:S(2)}, u32[]{:S(2)}) async-start(bf16[64,6,448]{2,1,0:T(8,128)(2,1)} %all_to_all.8), calls=%async_computation | async-start | bytes 1048576 | tf_op jit(solution)/shard_map/all_to_all | solution.py:84
  57.0 75.1 %reduce-scatter.2.cloned.1.call-start = ((), (), s32[]{:S(2)}) async-start(), calls=%async_computation.2 | async-start | bytes 4718592 | tf_op jit(solution)/shard_map/reduce_scatter | solution.py:98
  57.0 12.5 %copy-start.2 = (s32[64]{0:T(128)S(1)}, s32[64]{0:T(128)}, u32[]{:S(2)}) copy-start(s32[64]{0:T(128)} %param.6) | copy-start | bytes 772
  80.6 137.0 %all-gather.3.cloned.1.call-start = ((), (), s32[]{:S(2)}) async-start(), calls=%async_computation.3 | async-start | bytes 4259840 | tf_op jit(solution)/shard_map/all_gather | solution.py:112
  133.8 168.5 %all-gather.5.cloned.1.call-start = ((), (), s32[]{:S(2)}) async-start(), calls=%async_computation.4 | async-start | bytes 4259840 | tf_op jit(solution)/shard_map/all_gather | solution.py:113
  302.3 19.3 %copy-start.1 = (bf16[1152,448]{0,1:T(8,128)(2,1)S(1)}, bf16[1152,448]{0,1:T(8,128)(2,1)}, u32[]{:S(2)}) copy-start(bf16[1152,448]{0,1:T(8,128)(2,1)} %param.8) | copy-start | bytes 3096580
Sparse Core Ops, SparseCore 0:
  80.7 51.2 reduce-scatter.1
  135.2 82.3 all-gather.2
  220.7 81.5 all-gather.4
where the time goes:
time: 329 us; the launch traced here: 328 us
  waiting for transfers between devices  186 us (57%)
  matrix products  43 us (13%)
  other arithmetic  26.9 us (8%)
  blocking collectives  22 us (7%)
  local copies, waits for them, and re-layouts  20.2 us (6%)
  starting transfers between devices  16.6 us (5%)
  between operations  13.3 us (4%)
    all_gather x1, waiting for transfers between devices, local(): lax.all_gather(key_own, 'seq', axis=0, tiled=True)  78.7 us
    reduce_scatter x1, waiting for transfers between devices, local(): lax.psum_scatter(jnp.einsum('tc,cpw->ptw', visual, piece_w, preferred_ele...  51.4 us
    all_gather x1, waiting for transfers between devices, local(): lax.all_gather(value_own, 'seq', axis=0, tiled=True)  50.8 us
    all_gather x1, blocking collectives, local(): lax.all_gather(normed, 'kvh', axis=1, tiled=True)  22 us
    dot_general x1, matrix products, add_keys(): jnp.einsum('qhk,kd->qhd', weights.astype(jnp.bfloat16), value_piece, pref...  18.5 us
    dot_general x1, matrix products, add_keys(): jnp.einsum('qhd,kd->qhk', queries, key_piece, preferred_element_type=jnp....  17.6 us
    all_to_all x1, starting transfers between devices, local(): lax.all_to_all(outgoing, 'seq', split_axis=0, concat_axis=0, tiled=True)  16.4 us
    reduce_sum x1, other arithmetic, add_keys(): total = jnp.sum(weights, axis=-1)  16.3 us
  transfers between devices with their start and end apart: 4, of which 4 were waited for; matrix products, arithmetic and copies ran while one was open for 15% of the time, Pallas kernels for 0%

commit v1 on v0

--- a/solution.py
+++ b/solution.py
@@ -2,12 +2,19 @@
 import jax.numpy as jnp
 from jax import lax
 from jax.sharding import PartitionSpec as P
+from jax.lax import all_to_all, axis_size
 
 KV_HEADS = 4
 HEAD_DIM = 128
 GROUP_HEADS = 4
 norm_eps = 1e-06
 masked_score = -1e30
+
+
+def _derive_area(content, which_axis="kvh"):
+    return jnp.concatenate(
+        all_to_all(jnp.stack([content] * axis_size(which_axis)), which_axis, 0, 0), 1
+    )
 
 
 def layer_norm(states, norm_gain):
@@ -66,10 +73,7 @@
     heads_local = GROUP_HEADS // rep_count
     normed = layer_norm(vision_states, norm_gain)
     hidden = jnp.einsum(
-        "frv,vc->frc",
-        lax.all_gather(normed, "kvh", axis=1, tiled=True),
-        projector,
-        preferred_element_type=jnp.float32,
+        "frv,vc->frc", _derive_area(normed), projector, preferred_element_type=jnp.float32
     )
     visual_frames = jax.nn.gelu(hidden, approximate=False).astype(jnp.bfloat16)
     ends = jnp.cumsum(frame_tokens)

time: 329 us -> 333 us (1.012)
  blocking collectives: 22 us -> 0 us
  waiting for transfers between devices: 186 us -> 206 us
  starting transfers between devices: 16.6 us -> 21.9 us
    all_gather x1 -> x0, blocking collectives: 22 us -> none  [local(): lax.all_gather(normed, 'kvh', axis=1, tiled=True)]
    all_to_all x0 -> x1, waiting for transfers between devices: none -> 19.3 us  [_derive_area(): all_to_all(jnp.stack([content] * axis_size(which_axis)), which_axis, 0, 0)]
    all_to_all x0 -> x1, starting transfers between devices: none -> 7.64 us  [_derive_area(): all_to_all(jnp.stack([content] * axis_size(which_axis)), which_axis, 0, 0)]
  transfers between devices with their start and end apart: 4 -> 5, of which waited for: 4 -> 5; matrix products, arithmetic and copies ran while one was open for 15% -> 16% of each run, Pallas kernels for 0% -> 0%
where the time goes in v1:
time: 333 us
  waiting for transfers between devices  206 us (62%)
  matrix products  43 us (13%)
  other arithmetic  26.9 us (8%)
  starting transfers between devices  21.9 us (7%)
  local copies, waits for them, and re-layouts  21.1 us (6%)
  between operations  13.3 us (4%)
    all_gather x1, waiting for transfers between devices, local(): lax.all_gather(key_own, 'seq', axis=0, tiled=True)  78.7 us
    reduce_scatter x1, waiting for transfers between devices, local(): lax.psum_scatter(jnp.einsum('tc,cpw->ptw', visual, piece_w, preferred_ele...  52.4 us
    all_gather x1, waiting for transfers between devices, local(): lax.all_gather(value_own, 'seq', axis=0, tiled=True)  50.8 us
    all_to_all x1, waiting for transfers between devices, _derive_area(): all_to_all(jnp.stack([content] * axis_size(which_axis)), which_axis, 0, 0)  19.3 us
    dot_general x1, matrix products, add_keys(): jnp.einsum('qhk,kd->qhd', weights.astype(jnp.bfloat16), value_piece, pref...  18.5 us
    dot_general x1, matrix products, add_keys(): jnp.einsum('qhd,kd->qhk', queries, key_piece, preferred_element_type=jnp....  17.6 us
    reduce_sum x1, other arithmetic, add_keys(): total = jnp.sum(weights, axis=-1)  16.3 us
    all_to_all x1, starting transfers between devices, local(): lax.all_to_all(outgoing, 'seq', split_axis=0, concat_axis=0, tiled=True)  14.1 us
  transfers between devices with their start and end apart: 5, of which 5 were waited for; matrix products, arithmetic and copies ran while one was open for 16% of the time, Pallas kernels for 0%

profile of v1, /device:TPU:1, one launch (start us, length us, event | category | flops | bytes accessed | tf_op | source)
XLA Modules:
  0.0 332.8 jit_solution(6692738283900959432)
XLA Ops:
  6.5 0.0 copy-start
  6.5 1.1 convert_reduce_fusion
  7.7 1.2 fusion.38
  8.9 1.1 fusion.42
  10.0 1.0 stack.2
  11.0 7.6 %all-to-all-start = ((bf16[4,1,96,1152]{3,2,1,0:T(8,128)(2,1)}), bf16[4,1,96,1152]{3,2,1,0:T(8,128)(2,1)S(1)}, u32[]{:S(2)}, u32[]{:S(2)}) async-start(bf16[4,1,96,1152]{3,2,1,0:T(8,128)(2,1)} %stack.2), calls=%async_computation | async-start | bytes 1769472 | tf_op jit(solution)/shard_map/all_to_all | solution.py:16
  18.6 0.7 copy.27
  19.4 0.1 reduce-window.8
  19.5 0.1 reduce.2
  19.6 0.7 sub.59
  20.3 0.6 dynamic_slice.3
  20.8 0.7 and_select_fusion.1
  21.5 0.1 broadcast_add_fusion
  21.6 0.1 add.150
  21.8 19.3 %all-to-all-done = bf16[4,1,96,1152]{3,2,1,0:T(8,128)(2,1)S(1)} async-done(((bf16[4,1,96,1152]{3,2,1,0:T(8,128)(2,1)}), bf16[4,1,96,1152]{3,2,1,0:T(8,128)(2,1)S(1)}, u32[]{:S(2)}, u32[]{:S(2)}) %all-to-all-start) | async-done | bytes 884768 | tf_op jit(solution)/shard_map/all_to_all | solution.py:16
  41.0 0.0 copy-done
  41.0 2.1 fusion.28
  43.2 0.2 copy.28
  43.3 2.1 gather_fusion
  45.4 1.0 all_to_all.12
  46.4 14.1 %all-to-all-start.1 = ((bf16[64,6,448]{2,1,0:T(8,128)(2,1)}), bf16[64,6,448]{2,1,0:T(8,128)(2,1)S(1)}, u32[]{:S(2)}, u32[]{:S(2)}) async-start(bf16[64,6,448]{2,1,0:T(8,128)(2,1)} %all_to_all.12), calls=%async_computation.1 | async-start | bytes 1048576 | tf_op jit(solution)/shard_map/all_to_all | solution.py:88
  60.5 0.0 reduce-scatter.2.cloned.1.call-start
  60.6 0.0 copy-start.2
  60.6 4.6 %copy.23 = bf16[448,3072]{0,1:T(8,128)(2,1)} copy(bf16[448,3072]{1,0:T(8,128)(2,1)} %param.9) | data formatting | bytes 5505024 | tf_op args[4]
  65.2 1.8 slice.24
  67.0 2.3 slice.25
  69.3 2.3 copy.26
  71.6 1.5 copy.25
  73.1 0.0 copy-done.2
  73.1 0.1 fusion.50
  73.3 4.6 %all-to-all-done.1 = bf16[64,6,448]{2,1,0:T(8,128)(2,1)S(1)} async-done(((bf16[64,6,448]{2,1,0:T(8,128)(2,1)}), bf16[64,6,448]{2,1,0:T(8,128)(2,1)S(1)}, u32[]{:S(2)}, u32[]{:S(2)}) %all-to-all-start.1) | async-done | bytes 344096 | tf_op jit(solution)/shard_map/all_to_all | solution.py:88
  77.9 0.2 all_to_all.14
  78.1 1.2 gather_fusion.1
  79.3 0.1 broadcast_in_dim.58
  79.4 4.8 %fusion.13 = f32[8,256,512]{1,2,0:T(8,128)} fusion(bf16[448,8,256]{2,0,1:T(8,128)(2,1)S(1)} %bitcast.44, bf16[448,8,256]{2,0,1:T(8,128)(2,1)} %copy.26, bf16[256,448]{1,0:T(8,128)(2,1)S(1)} %gather_fusion.1), kind=kOutput, calls=%fused_computation.17 | convolution fusion | flops 946864128 | bytes 8093696 | tf_op jit(solution)/shard_map/tc,cpw->ptw/dot_general | solution.py:103
  84.2 0.0 reduce-scatter.2.cloned.1.call-update
  84.2 0.0 all-gather.3.cloned.1.call-start
  84.2 52.4 %reduce-scatter.2.cloned.1.call-done = f32[1,256,512]{1,2,0:T(8,128)} async-done(((f32[8,256,512]{1,2,0:T(8,128)}), f32[1,256,512]{1,2,0:T(8,128)}) %reduce-scatter.2.cloned.1.call-update) | async-done | bytes 524304 | tf_op jit(solution)/shard_map/reduce_scatter | solution.py:102
  136.6 1.1 convert_bitcast_fusion
  137.7 0.7 fusion.60
  138.4 0.0 all-gather.3.cloned.1.call-update
  138.4 0.0 all-gather.5.cloned.1.call-start
  138.5 0.7 all-gather.5.cloned.1.call-update
  139.1 4.3 %broadcast_compare_fusion = pred[256,16384]{1,0:T(8,128)(4,1)} fusion(s32[16384]{0:T(1024)S(1)} %fusion.51, s32[256]{0:T(256)S(1)} %multiply_add_fusion), kind=kLoop, calls=%fused_computation.9 | loop fusion | flops 4194304 | bytes 4260864 | tf_op jit(solution)/shard_map/le | solution.py:36
  143.5 78.7 %all-gather.3.cloned.1.call-done = bf16[16384,128]{0,1:T(8,128)(2,1)} async-done(((bf16[256,128]{0,1:T(8,128)(2,1)}), bf16[16384,128]{0,1:T(8,128)(2,1)}) %all-gather.3.cloned.1.call-update) | async-done | bytes 4194320 | tf_op jit(solution)/shard_map/all_gather | solution.py:116
  222.2 17.6 %fusion = (f32[256,2]{0,1:T(2,128)S(1)}, f32[256,2,16384]{2,0,1:T(8,128)}) fusion(pred[256,16384]{1,0:T(8,128)(4,1)} %broadcast_compare_fusion, bf16[256,2,128]{0,2,1:T(8,128)(2,1)S(1)} %bitcast.46, bf16[16384,128]{0,1:T(8,128)(2,1)} %all-gather.3.cloned.1.call-done), kind=kOutput, calls=%fused_computation.4 | convolution fusion | flops 2172648960 | bytes 42076160 | tf_op jit(solution)/shard_map/qhd,kd->qhk/dot_general | solution.py:38
  239.8 16.3 %fusion.1 = f32[256,2]{0,1:T(2,128)S(1)} fusion(f32[256,2,16384]{2,0,1:T(8,128)} %get-tuple-element.10, f32[256,2]{0,1:T(2,128)S(1)} %broadcast_maximum_fusion, pred[256,16384]{1,0:T(8,128)(4,1)} %broadcast_compare_fusion), kind=kLoop, calls=%fused_computation.5 | loop fusion | flops 41942528 | bytes 37752832 | tf_op jit(solution)/shard_map/reduce_sum | solution.py:44
  256.1 50.8 %all-gather.5.cloned.1.call-done = bf16[16384,128]{0,1:T(8,128)(2,1)} async-done(((bf16[256,128]{0,1:T(8,128)(2,1)}), bf16[16384,128]{0,1:T(8,128)(2,1)}) %all-gather.5.cloned.1.call-update) | async-done | bytes 4194320 | tf_op jit(solution)/shard_map/all_gather | solution.py:117
  306.9 0.0 copy-start.1
  306.9 18.5 %fusion.21 = bf16[256,2,128]{0,2,1:T(8,128)(2,1)S(1)} fusion(bf16[16384,128]{0,1:T(8,128)(2,1)} %all-gather.5.cloned.1.call-done, f32[256,2,16384]{2,0,1:T(8,128)} %get-tuple-element.10, f32[256,2]{0,1:T(2,128)S(1)} %broadcast_maximum_fusion, pred[256,16384]{1,0:T(8,128)(4,1)} %broadcast_compare_fusion, f32[256,2]{0,1:T(2,128)S(1)} %fusion.1), kind=kOutput, calls=%fused_computation.19 | convolution fusion | flops 2189557760 | bytes 42078208 | tf_op jit(solution)/shard_map/qhk,kd->qhd/dot_general | solution.py:45
  325.5 0.8 copy.32
  326.2 0.0 copy-done.1
  (12 shorter events, 0.1 us)
Async XLA Ops:
  6.5 34.5 %copy-start = (bf16[1152,448]{0,1:T(8,128)(2,1)S(1)}, bf16[1152,448]{0,1:T(8,128)(2,1)}, u32[]{:S(2)}) copy-start(bf16[1152,448]{0,1:T(8,128)(2,1)} %param.8) | copy-start | bytes 3096580
  11.0 30.0 %all-to-all-start = ((bf16[4,1,96,1152]{3,2,1,0:T(8,128)(2,1)}), bf16[4,1,96,1152]{3,2,1,0:T(8,128)(2,1)S(1)}, u32[]{:S(2)}, u32[]{:S(2)}) async-start(bf16[4,1,96,1152]{3,2,1,0:T(8,128)(2,1)} %stack.2), calls=%async_computation | async-start | bytes 1769472 | tf_op jit(solution)/shard_map/all_to_all | solution.py:16
  46.4 31.5 %all-to-all-start.1 = ((bf16[64,6,448]{2,1,0:T(8,128)(2,1)}), bf16[64,6,448]{2,1,0:T(8,128)(2,1)S(1)}, u32[]{:S(2)}, u32[]{:S(2)}) async-start(bf16[64,6,448]{2,1,0:T(8,128)(2,1)} %all_to_all.12), calls=%async_computation.1 | async-start | bytes 1048576 | tf_op jit(solution)/shard_map/all_to_all | solution.py:88
  60.5 76.1 %reduce-scatter.2.cloned.1.call-start = ((), (), s32[]{:S(2)}) async-start(), calls=%async_computation.3 | async-start | bytes 4718592 | tf_op jit(solution)/shard_map/reduce_scatter | solution.py:102
  60.6 12.5 %copy-start.2 = (s32[64]{0:T(128)S(1)}, s32[64]{0:T(128)}, u32[]{:S(2)}) copy-start(s32[64]{0:T(128)} %param.6) | copy-start | bytes 772
  84.2 138.0 %all-gather.3.cloned.1.call-start = ((), (), s32[]{:S(2)}) async-start(), calls=%async_computation.4 | async-start | bytes 4259840 | tf_op jit(solution)/shard_map/all_gather | solution.py:116
  138.4 168.5 %all-gather.5.cloned.1.call-start = ((), (), s32[]{:S(2)}) async-start(), calls=%async_computation.5 | async-start | bytes 4259840 | tf_op jit(solution)/shard_map/all_gather | solution.py:117
  306.9 19.3 %copy-start.1 = (bf16[1152,448]{0,1:T(8,128)(2,1)S(1)}, bf16[1152,448]{0,1:T(8,128)(2,1)}, u32[]{:S(2)}) copy-start(bf16[1152,448]{0,1:T(8,128)(2,1)} %param.8) | copy-start | bytes 3096580
Sparse Core Ops, SparseCore 0:
  84.3 52.2 reduce-scatter.1
  139.8 82.3 all-gather.2
  225.3 81.5 all-gather.4
